TPU v7x, 32 devices: a whole 2x2x4 slice. The times are simulated.
32 devices in a mesh: ctx: 16 (over z, x, core), head: 2 (over y).
Axes of the slice: x: 2, y: 2, z: 4, core: 2. Of those that a mesh axis runs over, the one named last changes fastest.
Arguments:
- queries: bfloat16 [8192, 1024], P('ctx', 'head'), may hold values from -6 to 6
- key_rows: bfloat16 [8192, 1024], P('ctx', 'head'), may hold values from -6 to 6
- values: bfloat16 [8192, 1024], P('ctx', 'head'), may hold values from -6 to 6
- outputs: bfloat16 [8192, 1024], P('ctx', 'head'), may hold values from -6 to 6
- out_grad: bfloat16 [8192, 1024], P('ctx', 'head'), may hold values from -48 to 48
- log_norm: bfloat16 [8, 8192], P('head', 'ctx'), may hold values from 4.5 to 7.5
- rand_blocks: int32 [64, 3], P('ctx'), may hold values from -1 to 61, as said below
Outputs:
- query_grad: bfloat16 [8192, 1024], P('ctx', 'head')
- key_grad: bfloat16 [8192, 1024], P('ctx', 'head')
- value_grad: bfloat16 [8192, 1024], P('ctx', 'head')
Inputs may be any that keep to these rules, and one draw needn't show every extreme that they name: `rand_blocks`: an entry of row j is a sequence block index of a key block for the query block of row j, or -1 for none. A named block lies between 1 and that query block's sequence index minus 2; the blocks named in the 4 rows of one index of ctx lie on distinct indices of ctx, none of them index 0.
All inputs are finite; a program needn't handle non-finite values.
Results may differ from a plain program's by a relative error of at most 0.0065.
Values may be sent and summed in bfloat16 or wider, within the bound.
No kernel may reach another device: no remote copies, remote signals or barrier semaphores. Data moves between devices by JAX's collectives and lax.ppermute only.
A program may use at most 128 MiB of HBM per device.

v0:
```python
import jax
import jax.numpy as jnp
from jax import lax
from jax.sharding import PartitionSpec as P

PAIR = 2
WINDOW = 2
GLOBAL = 1
RANDOM = 3


def padded(cells, sides, width):
    for axis, dim in sides:
        count = lax.axis_size(axis)
        ends = count - 1
        head = lax.slice_in_dim(cells, 0, width, axis=dim)
        tail = lax.slice_in_dim(cells, cells.shape[dim] - width, cells.shape[dim], axis=dim)
        cells = jnp.concatenate(
            [
                lax.ppermute(tail, axis, [(i, (i + 1) % count) for i in range(ends)]),
                cells,
                lax.ppermute(head, axis, [((i + 1) % count, i) for i in range(ends)]),
            ],
            axis=dim,
        )
    return cells


def spread_2(array, axis, root):
    mine = lax.axis_index(axis) == root
    return lax.psum(jnp.where(mine, array, jnp.zeros_like(array)), axis)


def pair_grads(query_heads, grad_heads, norm_blk, delta_blk, key_heads, value_heads, visible):
    head_size = query_heads.shape[-1]
    scaling = head_size ** (-0.5)
    scores = (
        jnp.einsum("nhid,nhjd->nhij", query_heads, key_heads, preferred_element_type=jnp.float32)
        * scaling
    )
    attn_prob = jnp.exp(scores - norm_blk.astype(jnp.float32)[:, :, :, None]) * visible[:, None]
    prob_low = attn_prob.astype(jnp.bfloat16)
    value_term = jnp.einsum(
        "nhij,nhid->nhjd", prob_low, grad_heads, preferred_element_type=jnp.float32
    )
    grad_prob = jnp.einsum(
        "nhid,nhjd->nhij", grad_heads, value_heads, preferred_element_type=jnp.float32
    )
    score_low = (attn_prob * (grad_prob - delta_blk.astype(jnp.float32)[:, :, :, None])).astype(
        jnp.bfloat16
    )
    query_term = (
        jnp.einsum("nhij,nhjd->nhid", score_low, key_heads, preferred_element_type=jnp.float32)
        * scaling
    )
    key_term = (
        jnp.einsum("nhij,nhid->nhjd", score_low, query_heads, preferred_element_type=jnp.float32)
        * scaling
    )
    return (query_term, key_term, value_term)


def shards(queries, key_rows, values, outputs, out_grad, log_norm, rand_blocks):
    ctx_size = lax.axis_size("ctx")
    my_index = lax.axis_index("ctx")
    row_count, features = queries.shape
    head_count = log_norm.shape[0]
    head_size = features // head_count
    slot_count = 2 * PAIR
    height = row_count // slot_count
    block_total = slot_count * ctx_size
    block_shape = (slot_count, head_count, height, head_size)

    def heads_major(array):
        return jnp.transpose(array.reshape(slot_count, height, head_count, head_size), (0, 2, 1, 3))

    query_blk = heads_major(queries)
    key_blk = heads_major(key_rows)
    value_blk = heads_major(values)
    output_blk = heads_major(outputs)
    grad_blk = heads_major(out_grad)
    norm_blk = jnp.transpose(log_norm.reshape(head_count, slot_count, height), (1, 0, 2))
    delta_blk = jnp.sum(
        grad_blk.astype(jnp.float32) * output_blk.astype(jnp.float32), axis=-1
    ).astype(jnp.bfloat16)
    within = jnp.arange(slot_count, dtype=jnp.int32)
    seq_blk = jnp.where(
        within < PAIR, PAIR * my_index + within, block_total - 1 - PAIR * my_index - (within - PAIR)
    )
    last_dev = my_index == ctx_size - 1
    first_dev = my_index == 0
    causal = jnp.tril(jnp.ones((height, height), jnp.float32))
    self_query, self_key, self_value = pair_grads(
        query_blk,
        grad_blk,
        norm_blk,
        delta_blk,
        key_blk,
        value_blk,
        jnp.broadcast_to(causal, (slot_count, height, height)),
    )
    rim_keys = jnp.stack(
        [
            jnp.stack([key_blk[PAIR], key_blk[PAIR - 1]]),
            jnp.stack([value_blk[PAIR], value_blk[PAIR - 1]]),
        ]
    )
    widened = padded(rim_keys, (("ctx", 1),), 1)
    tail_key = jnp.where(last_dev, key_blk[PAIR - 1], widened[0, 3])
    tail_value = jnp.where(last_dev, value_blk[PAIR - 1], widened[1, 3])
    prev_keys = jnp.concatenate(
        [widened[0, 0][None], key_blk[0 : PAIR - 1], key_blk[PAIR + 1 : slot_count], tail_key[None]]
    )
    prev_values = jnp.concatenate(
        [
            widened[1, 0][None],
            value_blk[0 : PAIR - 1],
            value_blk[PAIR + 1 : slot_count],
            tail_value[None],
        ]
    )
    visible = jnp.where((within == 0) & first_dev, 0.0, 1.0).astype(jnp.float32)[:, None, None]
    window_query, term_key, term_value = pair_grads(
        query_blk, grad_blk, norm_blk, delta_blk, prev_keys, prev_values, visible
    )
    out_rim = jnp.stack(
        [
            jnp.stack([term_key[0], term_key[slot_count - 1]]),
            jnp.stack([term_value[0], term_value[slot_count - 1]]),
        ]
    )
    came_back = padded(out_rim.astype(jnp.bfloat16), (("ctx", 1),), 1).astype(out_rim.dtype)
    own_tail = jnp.where(last_dev, 1.0, 0.0).astype(jnp.float32)

    def spread(term, returned):
        return jnp.concatenate(
            [
                term[1:PAIR],
                (term[slot_count - 1] * own_tail + returned[3])[None],
                returned[0][None],
                term[PAIR : slot_count - 1],
            ]
        )

    window_key = spread(term_key, came_back[0])
    window_value = spread(term_value, came_back[1])
    global_kv = spread_2(jnp.stack([key_blk[0:GLOBAL], value_blk[0:GLOBAL]]), "ctx", 0)
    target = jnp.repeat(jnp.arange(GLOBAL, dtype=jnp.int32), slot_count)
    visible_glob = (jnp.tile(seq_blk, GLOBAL) >= target + WINDOW).astype(jnp.float32)[:, None, None]
    glob_query, glob_key, glob_value = pair_grads(
        jnp.tile(query_blk, (GLOBAL, 1, 1, 1)),
        jnp.tile(grad_blk, (GLOBAL, 1, 1, 1)),
        jnp.tile(norm_blk, (GLOBAL, 1, 1)),
        jnp.tile(delta_blk, (GLOBAL, 1, 1)),
        jnp.repeat(global_kv[0], slot_count, axis=0),
        jnp.repeat(global_kv[1], slot_count, axis=0),
        visible_glob,
    )
    glob_query = jnp.sum(glob_query.reshape((GLOBAL,) + block_shape), axis=0)
    part_key = jnp.sum(glob_key.reshape((GLOBAL,) + block_shape), axis=1)
    part_value = jnp.sum(glob_value.reshape((GLOBAL,) + block_shape), axis=1)
    total_key, total_value = lax.psum((part_key, part_value), "ctx")
    owner_flag = jnp.where(first_dev, 1.0, 0.0).astype(jnp.float32)
    padding = jnp.zeros((slot_count - GLOBAL,) + block_shape[1:], jnp.float32)
    glob_key_add = jnp.concatenate([total_key * owner_flag, padding])
    glob_value_add = jnp.concatenate([total_value * owner_flag, padding])
    ref_valid = rand_blocks >= 0
    in_front = rand_blocks < block_total // 2
    mirror = block_total - 1 - rand_blocks
    owner_dev = jnp.where(in_front, rand_blocks // PAIR, mirror // PAIR)
    owner_dev = jnp.where(ref_valid, owner_dev, ctx_size).reshape(-1)
    key_slot = jnp.where(in_front, rand_blocks % PAIR, PAIR + mirror % PAIR) + 1
    key_slot = jnp.where(ref_valid, key_slot, 0).reshape(-1)
    targets = jnp.arange(ctx_size, dtype=jnp.int32)
    matches = owner_dev[None, :] == targets[:, None]
    slot_send = jnp.sum(jnp.where(matches, key_slot[None, :], 0), axis=1)
    key_flat = key_blk.reshape(slot_count, -1)
    value_flat = value_blk.reshape(slot_count, -1)
    slot_ids = jnp.arange(1, slot_count + 1, dtype=jnp.int32)
    select = jnp.any(matches.reshape(ctx_size, slot_count, RANDOM), axis=2).astype(jnp.bfloat16)

    def route_rows(block):
        return jnp.dot(
            select, block.reshape(slot_count, -1), preferred_element_type=jnp.float32
        ).astype(jnp.bfloat16)

    arrived = (
        lax.all_to_all(route_rows(query_blk), "ctx", split_axis=0, concat_axis=0, tiled=True),
        lax.all_to_all(route_rows(grad_blk), "ctx", split_axis=0, concat_axis=0, tiled=True),
        lax.all_to_all(route_rows(norm_blk), "ctx", split_axis=0, concat_axis=0, tiled=True),
        lax.all_to_all(route_rows(delta_blk), "ctx", split_axis=0, concat_axis=0, tiled=True),
        lax.all_to_all(slot_send, "ctx", split_axis=0, concat_axis=0, tiled=True),
    )
    group_size = 8
    rounds = ctx_size // group_size
    item_shape = (group_size,) + block_shape[1:]
    stat_shape = (group_size, head_count, height)

    def owner_step(carry, item):
        query_item, grad_item, norm_item, delta_item, slot_item = item
        choose = slot_item[:, None] == slot_ids[None, :]
        choose_low = choose.astype(jnp.bfloat16)
        key_item = (
            jnp.dot(choose_low, key_flat, preferred_element_type=jnp.float32)
            .astype(jnp.bfloat16)
            .reshape(item_shape)
        )
        value_item = (
            jnp.dot(choose_low, value_flat, preferred_element_type=jnp.float32)
            .astype(jnp.bfloat16)
            .reshape(item_shape)
        )
        visible_rand = (slot_item > 0).astype(jnp.float32)[:, None, None]
        term_query, term_key, term_value = pair_grads(
            query_item.reshape(item_shape),
            grad_item.reshape(item_shape),
            norm_item.reshape(stat_shape),
            delta_item.reshape(stat_shape),
            key_item,
            value_item,
            visible_rand,
        )
        choose_float = choose.astype(jnp.float32)
        key_acc = carry[0] + jnp.einsum(
            "gs,gx->sx",
            choose_float,
            term_key.reshape(group_size, -1),
            precision=lax.Precision.HIGHEST,
        )
        value_acc = carry[1] + jnp.einsum(
            "gs,gx->sx",
            choose_float,
            term_value.reshape(group_size, -1),
            precision=lax.Precision.HIGHEST,
        )
        return ((key_acc, value_acc), term_query.astype(jnp.bfloat16).reshape(group_size, -1))

    def regroup(array):
        return array.reshape((rounds, group_size) + array.shape[1:])

    zero_acc = jnp.zeros((slot_count, height * features), jnp.float32)
    (rand_key, rand_value), answers = lax.scan(
        owner_step,
        (zero_acc, zero_acc),
        (
            regroup(arrived[0]),
            regroup(arrived[1]),
            regroup(arrived[2]),
            regroup(arrived[3]),
            regroup(arrived[4]),
        ),
    )
    answers = answers.reshape(ctx_size, height * features)
    returned = lax.all_to_all(answers, "ctx", split_axis=0, concat_axis=0, tiled=True)
    rand_query = jnp.dot(select.T, returned, preferred_element_type=jnp.float32)
    query_total = self_query + window_query + glob_query + rand_query.reshape(block_shape)
    key_total = self_key + window_key + glob_key_add + rand_key.reshape(block_shape)
    value_total = self_value + window_value + glob_value_add + rand_value.reshape(block_shape)

    def rows_major(array):
        return jnp.transpose(array.astype(jnp.bfloat16), (0, 2, 1, 3)).reshape(row_count, features)

    return (rows_major(query_total), rows_major(key_total), rows_major(value_total))


def solution(mesh):
    return jax.shard_map(
        shards,
        mesh=mesh,
        in_specs=(
            P("ctx", "head"),
            P("ctx", "head"),
            P("ctx", "head"),
            P("ctx", "head"),
            P("ctx", "head"),
            P("head", "ctx"),
            P("ctx", None),
        ),
        out_specs=(P("ctx", "head"), P("ctx", "head"), P("ctx", "head")),
        check_vma=False,
    )
```

profile of v0, /device:TPU:1, one launch (start us, length us, event | category | flops | bytes accessed | tf_op | source)
XLA Modules:
  0.0 470.3 jit_solution(4784505163282766554)
XLA Ops:
  8.8 7.3 %all-to-all-start = ((s32[16,1,1]{2,1,0:T(1,128)}), s32[16,1,1]{2,1,0:T(1,128)S(1)}, u32[]{:S(2)}, u32[]{:S(2)}) async-start(s32[16,1,1]{2,1,0:T(1,128)} %copy.127), calls=%async_computation | async-start | bytes 16384 | tf_op jit(solution)/shard_map/all_to_all | solution.py:192
  21.9 5.6 %all-to-all-start.4 = ((bf16[16,2,256]{2,1,0:T(2,128)(2,1)}), bf16[16,2,256]{2,1,0:T(2,128)(2,1)S(1)}, u32[]{:S(2)}, u32[]{:S(2)}) async-start(bf16[16,2,256]{2,1,0:T(2,128)(2,1)} %reshape.287), calls=%async_computation.4 | async-start | bytes 32768 | tf_op jit(solution)/shard_map/all_to_all | solution.py:191
  29.0 4.3 all-to-all-done.4
  33.3 4.0 all-to-all-start.2
  41.0 4.0 reshape.285
  45.0 6.1 %all-to-all-start.3 = ((bf16[16,2,32768]{2,1,0:T(2,128)(2,1)}), bf16[16,2,32768]{2,1,0:T(2,128)(2,1)S(1)}, u32[]{:S(2)}, u32[]{:S(2)}) async-start(bf16[16,2,32768]{2,1,0:T(2,128)(2,1)} %reshape.285), calls=%async_computation.3 | async-start | bytes 4194304 | tf_op jit(solution)/shard_map/all_to_all | solution.py:189
  69.1 4.5 reduce.5
  73.6 4.0 reshape.281
  77.6 15.0 %all-to-all-done.3 = bf16[16,2,32768]{2,1,0:T(2,128)(2,1)S(1)} async-done(((bf16[16,2,32768]{2,1,0:T(2,128)(2,1)}), bf16[16,2,32768]{2,1,0:T(2,128)(2,1)S(1)}, u32[]{:S(2)}, u32[]{:S(2)}) %all-to-all-start.3) | async-done | bytes 2097184 | tf_op jit(solution)/shard_map/all_to_all | solution.py:189
  92.7 12.4 %all-to-all-start.1 = ((bf16[16,2,32768]{2,1,0:T(2,128)(2,1)}), bf16[16,2,32768]{2,1,0:T(2,128)(2,1)}, u32[]{:S(2)}, u32[]{:S(2)}) async-start(bf16[16,2,32768]{2,1,0:T(2,128)(2,1)} %reshape.281), calls=%async_computation.1 | async-start | bytes 4194304 | tf_op jit(solution)/shard_map/all_to_all | solution.py:188
  124.6 6.8 %reshape.286 = bf16[16,1,65536]{2,1,0:T(2,128)(2,1)} reshape(bf16[16,2,32768]{2,1,0:T(2,128)(2,1)S(1)} %all-to-all-done.3) | data formatting | bytes 4194304
  131.4 4.5 copy.278
  135.8 10.6 %all-to-all-done.1 = bf16[16,2,32768]{2,1,0:T(2,128)(2,1)} async-done(((bf16[16,2,32768]{2,1,0:T(2,128)(2,1)}), bf16[16,2,32768]{2,1,0:T(2,128)(2,1)}, u32[]{:S(2)}, u32[]{:S(2)}) %all-to-all-start.1) | async-done | bytes 2097184 | tf_op jit(solution)/shard_map/all_to_all | solution.py:188
  146.4 10.4 %reshape.282 = bf16[16,1,65536]{2,1,0:T(2,128)(2,1)} reshape(bf16[16,2,32768]{2,1,0:T(2,128)(2,1)} %all-to-all-done.1) | data formatting | bytes 4194304
  156.9 5.9 %copy.279 = bf16[16,1,65536]{2,0,1:T(8,128)(2,1)} copy(bf16[16,1,65536]{2,1,0:T(2,128)(2,1)} %reshape.282) | data formatting | bytes 4194304
  162.7 48.4 %while.15 = (s32[]{:T(128)}, f32[4,65536]{1,0:T(4,128)}, f32[4,65536]{1,0:T(4,128)}, bf16[2,8,65536]{2,1,0:T(8,128)(2,1)}, s32[2,8]{1,0:T(2,128)S(1)}, /*index=5...) while((s32[]{:T(128)}, f32[4,65536]{1,0:T(4,128)}, ...), condition=%wide.region_5.6_spmd.clone, body=%wide.region_4.5_spmd.clone.sunk | while | flops 737157248 | bytes 105006344 | solution.py:242
  177.0 4.4 convolution_add_fusion.7
  201.2 4.4 convolution_add_fusion.7
  211.2 3.8 reduce.9
  217.8 11.0 %all-to-all-start.5 = ((bf16[16,2,32768]{2,1,0:T(2,128)(2,1)}), bf16[16,2,32768]{2,1,0:T(2,128)(2,1)}, u32[]{:S(2)}, u32[]{:S(2)}) async-start(bf16[16,2,32768]{2,1,0:T(2,128)(2,1)} %reshape.289), calls=%async_computation.5 | async-start | bytes 4194304 | tf_op jit(solution)/shard_map/all_to_all | solution.py:254
  238.4 104.7 %all-reduce.6.cloned.1.call-done = bf16[2,1,4,128,128]{4,3,2,1,0:T(8,128)(2,1)} async-done(((bf16[2,1,4,128,128]{4,3,2,1,0:T(8,128)(2,1)}), bf16[2,1,4,128,128]{4,3,2,1,0:T(8,128)(2,1)}) %all-reduce.6.cloned.1.call-update) | async-done | bytes 262160 | tf_op jit(solution)/shard_map/psum | solution.py:31
  352.4 86.0 %all-reduce.8.cloned.1.call-done = (f32[1,4,128,128]{3,2,1,0:T(8,128)}, f32[1,4,128,128]{3,2,1,0:T(8,128)}) async-done(((f32[1,4,128,128]{3,2,1,0:T(8,128)}, f32[1,4,128,128]{3,2,1,0:T(8,128)}), (f32[1,4,128,128]{3,2,1,0:T(8,128)}, f32[1,4,128,128]{3,2,1,0:T(8,128)})) %all-reduce.8.cloned.1.call-update) | async-done | bytes 524304 | tf_op jit(solution)/shard_map/psum | solution.py:162
  444.6 10.4 %reshape.290 = bf16[16,1,65536]{2,1,0:T(2,128)(2,1)} reshape(bf16[16,2,32768]{2,1,0:T(2,128)(2,1)} %all-to-all-done.5) | data formatting | bytes 4194304
  455.1 4.5 copy.277
  (275 shorter events, 119.8 us)
Async XLA Ops:
  8.8 13.0 %all-to-all-start = ((s32[16,1,1]{2,1,0:T(1,128)}), s32[16,1,1]{2,1,0:T(1,128)S(1)}, u32[]{:S(2)}, u32[]{:S(2)}) async-start(s32[16,1,1]{2,1,0:T(1,128)} %copy.127), calls=%async_computation | async-start | bytes 16384 | tf_op jit(solution)/shard_map/all_to_all | solution.py:192
  16.3 11.2 %copy-start.54 = (bf16[4,512]{1,0:T(4,128)(2,1)S(1)}, bf16[4,512]{1,0:T(4,128)(2,1)}, u32[]{:S(2)}) copy-start(bf16[4,512]{1,0:T(4,128)(2,1)} %param.14) | copy-start | bytes 12292
  17.4 104.1 %copy-start.10 = (bf16[4,128,4,128]{3,2,1,0:T(4,128)(2,1)}, bf16[4,128,4,128]{3,2,1,0:T(4,128)(2,1)S(1)}, u32[]{:S(2)}) copy-start(bf16[4,128,4,128]{3,2,1,0:T(4,128)(2,1)S(1)} %reshape.242) | copy-start | bytes 1572868
  19.1 47.8 %copy-start.52 = (pred[16,4]{0,1:T(4,128)(4,1)}, pred[16,4]{0,1:T(4,128)(4,1)S(1)}, u32[]{:S(2)}) copy-start(pred[16,4]{0,1:T(4,128)(4,1)S(1)} %fusion.98) | copy-start | bytes 196
  21.9 11.4 %all-to-all-start.4 = ((bf16[16,2,256]{2,1,0:T(2,128)(2,1)}), bf16[16,2,256]{2,1,0:T(2,128)(2,1)S(1)}, u32[]{:S(2)}, u32[]{:S(2)}) async-start(bf16[16,2,256]{2,1,0:T(2,128)(2,1)} %reshape.287), calls=%async_computation.4 | async-start | bytes 32768 | tf_op jit(solution)/shard_map/all_to_all | solution.py:191
  33.3 11.8 %all-to-all-start.2 = ((bf16[16,2,256]{2,1,0:T(2,128)(2,1)}), bf16[16,2,256]{2,1,0:T(2,128)(2,1)S(1)}, u32[]{:S(2)}, u32[]{:S(2)}) async-start(bf16[16,2,256]{2,1,0:T(2,128)(2,1)} %reshape.283), calls=%async_computation.2 | async-start | bytes 32768 | tf_op jit(solution)/shard_map/all_to_all | solution.py:190
  45.0 47.6 %all-to-all-start.3 = ((bf16[16,2,32768]{2,1,0:T(2,128)(2,1)}), bf16[16,2,32768]{2,1,0:T(2,128)(2,1)S(1)}, u32[]{:S(2)}, u32[]{:S(2)}) async-start(bf16[16,2,32768]{2,1,0:T(2,128)(2,1)} %reshape.285), calls=%async_computation.3 | async-start | bytes 4194304 | tf_op jit(solution)/shard_map/all_to_all | solution.py:189
  58.3 57.5 %collective-permute-start.1 = (bf16[2,1,4,128,128]{4,3,2,1,0:T(8,128)(2,1)S(1)}, bf16[2,1,4,128,128]{4,3,2,1,0:T(8,128)(2,1)}, u32[]{:S(2)}, u32[]{:S(2)}) collective-permute-start(bf16[2,1,4,128,128]{4,3,2,1,0:T(8,128)(2,1)S(1)} %get-tuple-element.165), channel_id=1, source_target_pairs={{2,0},{4,2},{6,4},{8,6},{10,8},{12,10},{14,12},{16,14},{18,16},{20... | collective-permute-start | bytes 786440 | tf_op jit(solution)/shard_map/ppermute | solution.py:22
  60.3 59.0 %collective-permute-start = (bf16[2,1,4,128,128]{4,3,2,1,0:T(8,128)(2,1)}, bf16[2,1,4,128,128]{4,3,2,1,0:T(8,128)(2,1)}, u32[]{:S(2)}, u32[]{:S(2)}) collective-permute-start(bf16[2,1,4,128,128]{4,3,2,1,0:T(8,128)(2,1)} %get-tuple-element.164), channel_id=1, source_target_pairs={{0,2},{2,4},{4,6},{6,8},{8,10},{10,12},{12,14},{14,16},{16,18},{18... | collective-permute-start | bytes 786440 | tf_op jit(solution)/shard_map/ppermute | solution.py:20
  92.7 53.8 %all-to-all-start.1 = ((bf16[16,2,32768]{2,1,0:T(2,128)(2,1)}), bf16[16,2,32768]{2,1,0:T(2,128)(2,1)}, u32[]{:S(2)}, u32[]{:S(2)}) async-start(bf16[16,2,32768]{2,1,0:T(2,128)(2,1)} %reshape.281), calls=%async_computation.1 | async-start | bytes 4194304 | tf_op jit(solution)/shard_map/all_to_all | solution.py:188
  217.8 11.1 %copy-start.42 = (bf16[1,4,128,128]{3,2,1,0:T(8,128)(2,1)S(1)}, bf16[1,4,128,128]{3,2,1,0:T(8,128)(2,1)}, u32[]{:S(2)}) copy-start(bf16[1,4,128,128]{3,2,1,0:T(8,128)(2,1)} %get-tuple-element.146) | copy-start | bytes 393220
  217.8 11.1 %copy-start.43 = (bf16[1,4,128,128]{3,2,1,0:T(8,128)(2,1)S(1)}, bf16[1,4,128,128]{3,2,1,0:T(8,128)(2,1)}, u32[]{:S(2)}) copy-start(bf16[1,4,128,128]{3,2,1,0:T(8,128)(2,1)} %get-tuple-element.147) | copy-start | bytes 393220
  217.8 11.1 %copy-start.11 = (bf16[4,128,4,128]{3,2,1,0:T(4,128)(2,1)S(1)}, bf16[4,128,4,128]{3,2,1,0:T(4,128)(2,1)}, u32[]{:S(2)}) copy-start(bf16[4,128,4,128]{3,2,1,0:T(4,128)(2,1)} %copy-done.10) | copy-start | bytes 1572868
  217.8 11.1 %copy-start.35 = (f32[4,4,128,128]{3,2,1,0:T(8,128)S(1)}, f32[4,4,128,128]{3,2,1,0:T(8,128)}, u32[]{:S(2)}) copy-start(f32[4,4,128,128]{3,2,1,0:T(8,128)} %copy-done.34) | copy-start | bytes 3145732
  217.8 226.8 %all-to-all-start.5 = ((bf16[16,2,32768]{2,1,0:T(2,128)(2,1)}), bf16[16,2,32768]{2,1,0:T(2,128)(2,1)}, u32[]{:S(2)}, u32[]{:S(2)}) async-start(bf16[16,2,32768]{2,1,0:T(2,128)(2,1)} %reshape.289), calls=%async_computation.5 | async-start | bytes 4194304 | tf_op jit(solution)/shard_map/all_to_all | solution.py:254
  228.8 114.3 %all-reduce.6.cloned.1.call-start = ((), (), s32[]{:S(2)}) async-start(), calls=%async_computation.6 | async-start | bytes 524288 | tf_op jit(solution)/shard_map/psum | solution.py:31
  230.2 117.7 %collective-permute-start.2 = (bf16[2,1,4,128,128]{4,3,2,1,0:T(8,128)(2,1)}, bf16[2,1,4,128,128]{4,3,2,1,0:T(8,128)(2,1)}, u32[]{:S(2)}, u32[]{:S(2)}) collective-permute-start(bf16[2,1,4,128,128]{4,3,2,1,0:T(8,128)(2,1)} %get-tuple-element.150), channel_id=1, source_target_pairs={{0,2},{2,4},{4,6},{6,8},{8,10},{10,12},{12,14},{14,16},{16,18},{18... | collective-permute-start | bytes 786440 | tf_op jit(solution)/shard_map/ppermute | solution.py:20
  233.9 114.0 %collective-permute-start.3 = (bf16[2,1,4,128,128]{4,3,2,1,0:T(8,128)(2,1)}, bf16[2,1,4,128,128]{4,3,2,1,0:T(8,128)(2,1)}, u32[]{:S(2)}, u32[]{:S(2)}) collective-permute-start(bf16[2,1,4,128,128]{4,3,2,1,0:T(8,128)(2,1)} %get-tuple-element.151), channel_id=1, source_target_pairs={{2,0},{4,2},{6,4},{8,6},{10,8},{12,10},{14,12},{16,14},{18,16},{20... | collective-permute-start | bytes 786440 | tf_op jit(solution)/shard_map/ppermute | solution.py:22
  236.6 107.6 %copy-start.16 = (bf16[4,128,4,128]{3,2,1,0:T(4,128)(2,1)S(1)}, bf16[4,128,4,128]{3,2,1,0:T(4,128)(2,1)}, u32[]{:S(2)}) copy-start(bf16[4,128,4,128]{3,2,1,0:T(4,128)(2,1)} %reshape.239) | copy-start | bytes 1572868
  236.6 107.6 %copy-start.57 = (f32[4,4,128]{2,1,0:T(4,128)S(1)}, f32[4,4,128]{2,1,0:T(4,128)}, u32[]{:S(2)}) copy-start(f32[4,4,128]{2,1,0:T(4,128)} %copy-done.55) | copy-start | bytes 24580
  236.6 108.7 %copy-start.51 = (f32[4,4,128]{2,1,0:T(4,128)S(1)}, f32[4,4,128]{2,1,0:T(4,128)}, u32[]{:S(2)}) copy-start(f32[4,4,128]{2,1,0:T(4,128)} %copy-done.49) | copy-start | bytes 24580
  236.6 201.9 %all-reduce.8.cloned.1.call-start = ((), (), s32[]{:S(2)}) async-start(), calls=%async_computation.7 | async-start | bytes 1048576 | tf_op jit(solution)/shard_map/psum | solution.py:162
  349.7 90.9 %copy-start.9 = (f32[4,65536]{1,0:T(4,128)S(1)}, f32[4,65536]{1,0:T(4,128)}, u32[]{:S(2)}) copy-start(f32[4,65536]{1,0:T(4,128)} %get-tuple-element.69) | copy-start | bytes 3145732
  352.4 88.2 %copy-start.31 = (f32[1,4,128,128]{3,2,1,0:T(8,128)S(1)}, f32[1,4,128,128]{3,2,1,0:T(8,128)}, u32[]{:S(2)}) copy-start(f32[1,4,128,128]{3,2,1,0:T(8,128)} %get-tuple-element.138) | copy-start | bytes 786436
  (57 other events, 161.2 us)
Sparse Core Ops, SparseCore 0:
  236.7 106.3 all-reduce.5
  348.0 90.4 all-reduce.7
where the time goes:
time: 479 us; the launch traced here: 470 us
  waiting for transfers between devices  221 us (46%)
  local copies, waits for them, and re-layouts  98.1 us (20%)
  starting transfers between devices  57.8 us (12%)
  matrix products  49.5 us (10%)
  other arithmetic  27.9 us (6%)
  between operations  15.2 us (3%)
    psum x1, waiting for transfers between devices, spread_2(): return lax.psum(jnp.where(mine, array, jnp.zeros_like(array)), axis)  105 us
    psum x1, waiting for transfers between devices, shards(): total_key, total_value = lax.psum((part_key, part_value), 'ctx')  86 us
    unnamed x119, local copies, waits for them, and re-layouts  61.9 us
    all_to_all x1, waiting for transfers between devices, shards(): lax.all_to_all(route_rows(grad_blk), 'ctx', split_axis=0, concat_axis=0,...  15 us
    all_to_all x1, starting transfers between devices, shards(): lax.all_to_all(route_rows(query_blk), 'ctx', split_axis=0, concat_axis=0,...  12.4 us
    all_to_all x1, starting transfers between devices, shards(): lax.all_to_all(answers, 'ctx', split_axis=0, concat_axis=0, tiled=True)  11 us
    all_to_all x1, waiting for transfers between devices, shards(): lax.all_to_all(route_rows(query_blk), 'ctx', split_axis=0, concat_axis=0,...  10.6 us
    reshape x8, local copies, waits for them, and re-layouts, heads_major(): array.reshape(slot_count, height, head_count, head_size)  9.61 us
  transfers between devices with their start and end apart: 12, of which 6 were waited for; matrix products, arithmetic and copies ran while one was open for 17% of the time, Pallas kernels for 0%

commit v1 on v0

--- a/solution.py
+++ b/solution.py
@@ -28,7 +28,7 @@
 
 def spread_2(array, axis, root):
     mine = lax.axis_index(axis) == root
-    return lax.psum(jnp.where(mine, array, jnp.zeros_like(array)), axis)
+    return jnp.sum(lax.all_gather(jnp.where(mine, array, jnp.zeros_like(array)), axis), axis=0)
 
 
 def pair_grads(query_heads, grad_heads, norm_blk, delta_blk, key_heads, value_heads, visible):

time: 479 us -> 434 us (0.906)
  waiting for transfers between devices: 221 us -> 175 us
  starting transfers between devices: 57.8 us -> 65.6 us
  local copies, waits for them, and re-layouts: 98.1 us -> 91.1 us
    psum x1 -> x0, waiting for transfers between devices: 105 us -> none  [spread_2(): return lax.psum(jnp.where(mine, array, jnp.zeros_like(array)), axis)]
    all_to_all x1, waiting for transfers between devices: 10.6 us -> 28.9 us  [shards(): lax.all_to_all(route_rows(query_blk), 'ctx', split_axis=0, concat_axis=0,...]
    all_to_all x1, waiting for transfers between devices: 0.01 us -> 17.5 us  [shards(): lax.all_to_all(answers, 'ctx', split_axis=0, concat_axis=0, tiled=True)]
    psum x1, waiting for transfers between devices: 86 us -> 101 us  [shards(): total_key, total_value = lax.psum((part_key, part_value), 'ctx')]
    all_to_all x1, starting transfers between devices: 11 us -> 18.9 us  [shards(): lax.all_to_all(answers, 'ctx', split_axis=0, concat_axis=0, tiled=True)]
    unnamed x119 -> x89, local copies, waits for them, and re-layouts: 61.9 us -> 60.4 us
  transfers between devices with their start and end apart: 12 -> 12, of which waited for: 6 -> 8; matrix products, arithmetic and copies ran while one was open for 17% -> 35% of each run, Pallas kernels for 0% -> 0%
where the time goes in v1:
time: 434 us; the launch traced here: 425 us
  waiting for transfers between devices  175 us (40%)
  local copies, waits for them, and re-layouts  91.1 us (21%)
  starting transfers between devices  65.6 us (15%)
  matrix products  48.6 us (11%)
  other arithmetic  29 us (7%)
  between operations  15 us (3%)
    psum x1, waiting for transfers between devices, shards(): total_key, total_value = lax.psum((part_key, part_value), 'ctx')  101 us
    unnamed x89, local copies, waits for them, and re-layouts  60.4 us
    all_to_all x1, waiting for transfers between devices, shards(): lax.all_to_all(route_rows(query_blk), 'ctx', split_axis=0, concat_axis=0,...  28.9 us
    all_to_all x1, starting transfers between devices, shards(): lax.all_to_all(answers, 'ctx', split_axis=0, concat_axis=0, tiled=True)  18.9 us
    all_to_all x1, waiting for transfers between devices, shards(): lax.all_to_all(answers, 'ctx', split_axis=0, concat_axis=0, tiled=True)  17.5 us
    all_to_all x1, waiting for transfers between devices, shards(): lax.all_to_all(route_rows(grad_blk), 'ctx', split_axis=0, concat_axis=0,...  17.3 us
    all_to_all x1, starting transfers between devices, shards(): lax.all_to_all(route_rows(query_blk), 'ctx', split_axis=0, concat_axis=0,...  11.7 us
    dot_general x2, matrix products, owner_step(): jnp.einsum('gs,gx->sx', choose_float, term_key.reshape(group_size, -1), p...  8.85 us
  transfers between devices with their start and end apart: 12, of which 8 were waited for; matrix products, arithmetic and copies ran while one was open for 35% of the time, Pallas kernels for 0%

profile of v1, /device:TPU:1, one launch (start us, length us, event | category | flops | bytes accessed | tf_op | source)
XLA Modules:
  0.0 425.1 jit_solution(12646689609900593393)
XLA Ops:
  8.8 7.3 %all-to-all-start = ((s32[16,1,1]{2,1,0:T(1,128)}), s32[16,1,1]{2,1,0:T(1,128)S(1)}, u32[]{:S(2)}, u32[]{:S(2)}) async-start(s32[16,1,1]{2,1,0:T(1,128)} %copy.127), calls=%async_computation | async-start | bytes 16384 | tf_op jit(solution)/shard_map/all_to_all | solution.py:192
  21.9 5.6 %all-to-all-start.4 = ((bf16[16,2,256]{2,1,0:T(2,128)(2,1)}), bf16[16,2,256]{2,1,0:T(2,128)(2,1)S(1)}, u32[]{:S(2)}, u32[]{:S(2)}) async-start(bf16[16,2,256]{2,1,0:T(2,128)(2,1)} %reshape.296), calls=%async_computation.4 | async-start | bytes 32768 | tf_op jit(solution)/shard_map/all_to_all | solution.py:191
  29.1 4.3 %all-to-all-done.4 = bf16[16,2,256]{2,1,0:T(2,128)(2,1)S(1)} async-done(((bf16[16,2,256]{2,1,0:T(2,128)(2,1)}), bf16[16,2,256]{2,1,0:T(2,128)(2,1)S(1)}, u32[]{:S(2)}, u32[]{:S(2)}) %all-to-all-start.4) | async-done | bytes 16416 | tf_op jit(solution)/shard_map/all_to_all | solution.py:191
  33.3 4.0 all-to-all-start.2
  41.1 4.0 reshape.294
  45.1 6.2 %all-to-all-start.3 = ((bf16[16,2,32768]{2,1,0:T(2,128)(2,1)}), bf16[16,2,32768]{2,1,0:T(2,128)(2,1)S(1)}, u32[]{:S(2)}, u32[]{:S(2)}) async-start(bf16[16,2,32768]{2,1,0:T(2,128)(2,1)} %reshape.294), calls=%async_computation.3 | async-start | bytes 4194304 | tf_op jit(solution)/shard_map/all_to_all | solution.py:189
  67.1 4.5 %reduce.7 = bf16[16,65536]{1,0:T(8,128)(2,1)} reduce(bf16[16,1,65536]{2,0,1:T(8,128)(2,1)} %fusion.24, bf16[]{:T(256)} %broadcast.231), dimensions={1}, to_apply=%copy.128.reduce_sub_computation | reduce | bytes 4194306 | tf_op jit(solution)/shard_map/all_to_all | solution.py:188
  71.6 4.0 reshape.290
  75.5 17.3 %all-to-all-done.3 = bf16[16,2,32768]{2,1,0:T(2,128)(2,1)S(1)} async-done(((bf16[16,2,32768]{2,1,0:T(2,128)(2,1)}), bf16[16,2,32768]{2,1,0:T(2,128)(2,1)S(1)}, u32[]{:S(2)}, u32[]{:S(2)}) %all-to-all-start.3) | async-done | bytes 2097184 | tf_op jit(solution)/shard_map/all_to_all | solution.py:189
  92.8 11.7 %all-to-all-start.1 = ((bf16[16,2,32768]{2,1,0:T(2,128)(2,1)}), bf16[16,2,32768]{2,1,0:T(2,128)(2,1)}, u32[]{:S(2)}, u32[]{:S(2)}) async-start(bf16[16,2,32768]{2,1,0:T(2,128)(2,1)} %reshape.290), calls=%async_computation.1 | async-start | bytes 4194304 | tf_op jit(solution)/shard_map/all_to_all | solution.py:188
  114.2 6.8 %reshape.295 = bf16[16,1,65536]{2,1,0:T(2,128)(2,1)} reshape(bf16[16,2,32768]{2,1,0:T(2,128)(2,1)S(1)} %all-to-all-done.3) | data formatting | bytes 4194304
  121.1 4.6 %copy.278 = bf16[16,1,65536]{2,0,1:T(8,128)(2,1)S(1)} copy(bf16[16,1,65536]{2,1,0:T(2,128)(2,1)} %reshape.295) | data formatting | bytes 4194304
  125.7 28.9 %all-to-all-done.1 = bf16[16,2,32768]{2,1,0:T(2,128)(2,1)} async-done(((bf16[16,2,32768]{2,1,0:T(2,128)(2,1)}), bf16[16,2,32768]{2,1,0:T(2,128)(2,1)}, u32[]{:S(2)}, u32[]{:S(2)}) %all-to-all-start.1) | async-done | bytes 2097184 | tf_op jit(solution)/shard_map/all_to_all | solution.py:188
  154.5 10.6 %reshape.291 = bf16[16,1,65536]{2,1,0:T(2,128)(2,1)} reshape(bf16[16,2,32768]{2,1,0:T(2,128)(2,1)} %all-to-all-done.1) | data formatting | bytes 4194304
  165.1 5.8 %copy.279 = bf16[16,1,65536]{2,0,1:T(8,128)(2,1)} copy(bf16[16,1,65536]{2,1,0:T(2,128)(2,1)} %reshape.291) | data formatting | bytes 4194304
  170.9 50.5 %while.15 = (s32[]{:T(128)}, f32[4,65536]{1,0:T(4,128)}, f32[4,65536]{1,0:T(4,128)}, bf16[2,8,65536]{2,1,0:T(8,128)(2,1)}, s32[2,8]{1,0:T(2,128)}, /*index=5*/bf...) while((s32[]{:T(128)}, f32[4,65536]{1,0:T(4,128)}, ...), condition=%wide.region_5.6_spmd.clone, body=%wide.region_4.5_spmd.clone.sunk | while | flops 737157248 | bytes 105006344 | solution.py:242
  186.3 4.4 %convolution_add_fusion.7 = f32[4,65536]{1,0:T(4,128)S(1)} fusion(f32[1,8,512,128]{3,2,1,0:T(8,128)} %bitcast.274, f32[4,65536]{1,0:T(4,128)S(1)} %copy-done.4, pred[]{:T(512)S(6)} %compare.11, s32[4]{0:T(128)S(1)} %iota_add_fusion.2, s32[8]{0:T(128)S(1)} %get-tuple-element.256), kind=kOutput, calls=%fused_computation.4.clone.1 | convolution fusion | flops 25690144 | bytes 4194353 | tf_op jit(solution)/shard_map/while/body/eval_jaxpr/gs,gx->sx/dot_general | solution.py:224
  211.5 4.4 %convolution_add_fusion.7 = f32[4,65536]{1,0:T(4,128)S(1)} fusion(f32[1,8,512,128]{3,2,1,0:T(8,128)} %bitcast.274, f32[4,65536]{1,0:T(4,128)S(1)} %copy-done.4, pred[]{:T(512)S(6)} %compare.11, s32[4]{0:T(128)S(1)} %iota_add_fusion.2, s32[8]{0:T(128)S(1)} %get-tuple-element.256), kind=kOutput, calls=%fused_computation.4.clone.1 | convolution fusion | flops 25690144 | bytes 4194353 | tf_op jit(solution)/shard_map/while/body/eval_jaxpr/gs,gx->sx/dot_general | solution.py:224
  221.4 3.8 reduce.11
  228.0 18.9 %all-to-all-start.5 = ((bf16[16,2,32768]{2,1,0:T(2,128)(2,1)}), bf16[16,2,32768]{2,1,0:T(2,128)(2,1)S(1)}, u32[]{:S(2)}, u32[]{:S(2)}) async-start(bf16[16,2,32768]{2,1,0:T(2,128)(2,1)} %reshape.298), calls=%async_computation.5 | async-start | bytes 4194304 | tf_op jit(solution)/shard_map/all_to_all | solution.py:254
  270.9 17.5 %all-to-all-done.5 = bf16[16,2,32768]{2,1,0:T(2,128)(2,1)S(1)} async-done(((bf16[16,2,32768]{2,1,0:T(2,128)(2,1)}), bf16[16,2,32768]{2,1,0:T(2,128)(2,1)S(1)}, u32[]{:S(2)}, u32[]{:S(2)}) %all-to-all-start.5) | async-done | bytes 2097184 | tf_op jit(solution)/shard_map/all_to_all | solution.py:254
  288.4 6.8 %reshape.299 = bf16[16,1,65536]{2,1,0:T(2,128)(2,1)} reshape(bf16[16,2,32768]{2,1,0:T(2,128)(2,1)S(1)} %all-to-all-done.5) | data formatting | bytes 4194304
  295.2 4.5 %copy.277 = bf16[16,1,65536]{2,0,1:T(8,128)(2,1)S(1)} copy(bf16[16,1,65536]{2,1,0:T(2,128)(2,1)} %reshape.299) | data formatting | bytes 4194304
  311.4 100.6 %all-reduce.5.cloned.1.call-done = (f32[1,4,128,128]{3,2,1,0:T(8,128)}, f32[1,4,128,128]{3,2,1,0:T(8,128)}) async-done(((f32[1,4,128,128]{3,2,1,0:T(8,128)}, f32[1,4,128,128]{3,2,1,0:T(8,128)}), (f32[1,4,128,128]{3,2,1,0:T(8,128)}, f32[1,4,128,128]{3,2,1,0:T(8,128)})) %all-reduce.5.cloned.1.call-update) | async-done | bytes 524304 | tf_op jit(solution)/shard_map/psum | solution.py:162
  (246 shorter events, 123.0 us)
Async XLA Ops:
  8.8 13.0 %all-to-all-start = ((s32[16,1,1]{2,1,0:T(1,128)}), s32[16,1,1]{2,1,0:T(1,128)S(1)}, u32[]{:S(2)}, u32[]{:S(2)}) async-start(s32[16,1,1]{2,1,0:T(1,128)} %copy.127), calls=%async_computation | async-start | bytes 16384 | tf_op jit(solution)/shard_map/all_to_all | solution.py:192
  16.3 11.3 %copy-start.38 = (bf16[4,512]{1,0:T(4,128)(2,1)S(1)}, bf16[4,512]{1,0:T(4,128)(2,1)}, u32[]{:S(2)}) copy-start(bf16[4,512]{1,0:T(4,128)(2,1)} %param.14) | copy-start | bytes 12292
  17.4 10.4 %copy-start.10 = (bf16[4,128,4,128]{3,2,1,0:T(4,128)(2,1)}, bf16[4,128,4,128]{3,2,1,0:T(4,128)(2,1)S(1)}, u32[]{:S(2)}) copy-start(bf16[4,128,4,128]{3,2,1,0:T(4,128)(2,1)S(1)} %reshape.251) | copy-start | bytes 1572868
  19.1 45.8 %copy-start.36 = (pred[16,4]{0,1:T(4,128)(4,1)}, pred[16,4]{0,1:T(4,128)(4,1)S(1)}, u32[]{:S(2)}) copy-start(pred[16,4]{0,1:T(4,128)(4,1)S(1)} %fusion.98) | copy-start | bytes 196
  21.9 11.5 %all-to-all-start.4 = ((bf16[16,2,256]{2,1,0:T(2,128)(2,1)}), bf16[16,2,256]{2,1,0:T(2,128)(2,1)S(1)}, u32[]{:S(2)}, u32[]{:S(2)}) async-start(bf16[16,2,256]{2,1,0:T(2,128)(2,1)} %reshape.296), calls=%async_computation.4 | async-start | bytes 32768 | tf_op jit(solution)/shard_map/all_to_all | solution.py:191
  33.3 11.7 %all-to-all-start.2 = ((bf16[16,2,256]{2,1,0:T(2,128)(2,1)}), bf16[16,2,256]{2,1,0:T(2,128)(2,1)S(1)}, u32[]{:S(2)}, u32[]{:S(2)}) async-start(bf16[16,2,256]{2,1,0:T(2,128)(2,1)} %reshape.292), calls=%async_computation.2 | async-start | bytes 32768 | tf_op jit(solution)/shard_map/all_to_all | solution.py:190
  45.1 6.2 %copy-start.27 = (bf16[512,512]{1,0:T(8,128)(2,1)S(1)}, bf16[512,512]{1,0:T(8,128)(2,1)}, u32[]{:S(2)}) copy-start(bf16[512,512]{1,0:T(8,128)(2,1)} %param.10) | copy-start | bytes 1572868
  45.1 47.7 %all-to-all-start.3 = ((bf16[16,2,32768]{2,1,0:T(2,128)(2,1)}), bf16[16,2,32768]{2,1,0:T(2,128)(2,1)S(1)}, u32[]{:S(2)}, u32[]{:S(2)}) async-start(bf16[16,2,32768]{2,1,0:T(2,128)(2,1)} %reshape.294), calls=%async_computation.3 | async-start | bytes 4194304 | tf_op jit(solution)/shard_map/all_to_all | solution.py:189
  56.2 54.6 %collective-permute-start.1 = (bf16[2,1,4,128,128]{4,3,2,1,0:T(8,128)(2,1)S(1)}, bf16[2,1,4,128,128]{4,3,2,1,0:T(8,128)(2,1)}, u32[]{:S(2)}, u32[]{:S(2)}) collective-permute-start(bf16[2,1,4,128,128]{4,3,2,1,0:T(8,128)(2,1)S(1)} %get-tuple-element.165), channel_id=1, source_target_pairs={{2,0},{4,2},{6,4},{8,6},{10,8},{12,10},{14,12},{16,14},{18,16},{20... | collective-permute-start | bytes 786440 | tf_op jit(solution)/shard_map/ppermute | solution.py:22
  58.2 191.8 %collective-permute-start = (bf16[2,1,4,128,128]{4,3,2,1,0:T(8,128)(2,1)}, bf16[2,1,4,128,128]{4,3,2,1,0:T(8,128)(2,1)}, u32[]{:S(2)}, u32[]{:S(2)}) collective-permute-start(bf16[2,1,4,128,128]{4,3,2,1,0:T(8,128)(2,1)} %get-tuple-element.164), channel_id=1, source_target_pairs={{0,2},{2,4},{4,6},{6,8},{8,10},{10,12},{12,14},{14,16},{16,18},{18... | collective-permute-start | bytes 786440 | tf_op jit(solution)/shard_map/ppermute | solution.py:20
  92.8 61.7 %all-to-all-start.1 = ((bf16[16,2,32768]{2,1,0:T(2,128)(2,1)}), bf16[16,2,32768]{2,1,0:T(2,128)(2,1)}, u32[]{:S(2)}, u32[]{:S(2)}) async-start(bf16[16,2,32768]{2,1,0:T(2,128)(2,1)} %reshape.290), calls=%async_computation.1 | async-start | bytes 4194304 | tf_op jit(solution)/shard_map/all_to_all | solution.py:188
  104.5 197.2 %all-gather.2.cloned.1.call-start = ((), (), s32[]{:S(2)}) async-start(), calls=%async_computation.6 | async-start | bytes 4456448 | tf_op jit(solution)/shard_map/all_gather | solution.py:31
  186.3 4.4 %copy-start.1 = (f32[8,4,128,128]{3,2,1,0:T(8,128)S(1)}, f32[8,4,128,128]{3,2,1,0:T(8,128)}, u32[]{:S(2)}) copy-start(f32[8,4,128,128]{3,2,1,0:T(8,128)} %copy-done) | copy-start | bytes 6291460 | tf_op jit(solution)/shard_map/while
  192.3 3.9 copy-start.13
  211.5 4.4 %copy-start.1 = (f32[8,4,128,128]{3,2,1,0:T(8,128)S(1)}, f32[8,4,128,128]{3,2,1,0:T(8,128)}, u32[]{:S(2)}) copy-start(f32[8,4,128,128]{3,2,1,0:T(8,128)} %copy-done) | copy-start | bytes 6291460 | tf_op jit(solution)/shard_map/while
  217.5 3.9 copy-start.13
  228.0 19.2 %copy-start.39 = (bf16[4,512]{1,0:T(4,128)(2,1)S(1)}, bf16[4,512]{1,0:T(4,128)(2,1)}, u32[]{:S(2)}) copy-start(bf16[4,512]{1,0:T(4,128)(2,1)} %param.14) | copy-start | bytes 12292
  228.0 60.4 %all-to-all-start.5 = ((bf16[16,2,32768]{2,1,0:T(2,128)(2,1)}), bf16[16,2,32768]{2,1,0:T(2,128)(2,1)S(1)}, u32[]{:S(2)}, u32[]{:S(2)}) async-start(bf16[16,2,32768]{2,1,0:T(2,128)(2,1)} %reshape.298), calls=%async_computation.5 | async-start | bytes 4194304 | tf_op jit(solution)/shard_map/all_to_all | solution.py:254
  246.9 165.0 %all-reduce.5.cloned.1.call-start = ((), (), s32[]{:S(2)}) async-start(), calls=%async_computation.7 | async-start | bytes 1048576 | tf_op jit(solution)/shard_map/psum | solution.py:162
  247.2 3.8 copy-start.40
  253.0 9.6 %collective-permute-start.2 = (bf16[2,1,4,128,128]{4,3,2,1,0:T(8,128)(2,1)S(1)}, bf16[2,1,4,128,128]{4,3,2,1,0:T(8,128)(2,1)S(1)}, u32[]{:S(2)}, u32[]{:S(2)}) collective-permute-start(bf16[2,1,4,128,128]{4,3,2,1,0:T(8,128)(2,1)S(1)} %get-tuple-element.150), channel_id=1, source_target_pairs={{0,2},{2,4},{4,6},{6,8},{8,10},{10,12},{12,14},{14,16},{16,18},{18... | collective-permute-start | bytes 786440 | tf_op jit(solution)/shard_map/ppermute | solution.py:20
  256.5 9.7 %collective-permute-start.3 = (bf16[2,1,4,128,128]{4,3,2,1,0:T(8,128)(2,1)S(1)}, bf16[2,1,4,128,128]{4,3,2,1,0:T(8,128)(2,1)S(1)}, u32[]{:S(2)}, u32[]{:S(2)}) collective-permute-start(bf16[2,1,4,128,128]{4,3,2,1,0:T(8,128)(2,1)S(1)} %get-tuple-element.151), channel_id=1, source_target_pairs={{2,0},{4,2},{6,4},{8,6},{10,8},{12,10},{14,12},{16,14},{18,16},{20... | collective-permute-start | bytes 786440 | tf_op jit(solution)/shard_map/ppermute | solution.py:22
  310.1 102.9 %copy-start.21 = (f32[4,4,128,128]{3,2,1,0:T(8,128)S(1)}, f32[4,4,128,128]{3,2,1,0:T(8,128)}, u32[]{:S(2)}) copy-start(f32[4,4,128,128]{3,2,1,0:T(8,128)} %copy-done.20) | copy-start | bytes 3145732
  310.1 102.9 %copy-start.22 = (f32[1,4,512,128]{3,2,1,0:T(8,128)S(1)}, f32[1,4,512,128]{3,2,1,0:T(8,128)}, u32[]{:S(2)}) copy-start(f32[1,4,512,128]{3,2,1,0:T(8,128)} %copy.166) | copy-start | bytes 3145732
  (42 other events, 81.4 us)
Sparse Core Ops, SparseCore 0:
  114.4 67.5 all-gather.1
  308.7 103.1 all-reduce.4
